TPU v7x, 256 devices: a whole 4x4x8 slice. The times are simulated.
256 devices in a mesh: kv: 8 (over z), blk: 32 (over y, x, core).
Axes of the slice: x: 4, y: 4, z: 8, core: 2. Of those that a mesh axis runs over, the one named last changes fastest.
Arguments:
- hidden_in: bfloat16 [4, 16, 4096], P(None, None, 'blk'), may hold values from -6 to 6
- attn_gain: bfloat16 [4096], P('blk'), may hold values from 0.5 to 1.5
- ffn_gain: bfloat16 [4096], replicated, may hold values from 0.5 to 1.5
- query_key_value_weight: bfloat16 [4096, 8, 768], P('blk', 'kv'), may hold values from -0.09375 to 0.09375
- out_weight: bfloat16 [4096, 4096], P('kv', 'blk'), may hold values from -0.09375 to 0.09375
- router_weight: bfloat16 [4096, 8], replicated, may hold values from -0.09375 to 0.09375
- expert_in: bfloat16 [8, 4096, 2, 8192], P('kv', None, None, 'blk'), may hold values from -0.09375 to 0.09375
- expert_down: bfloat16 [8, 8192, 4096], P('kv', 'blk'), may hold values from -0.125 to 0.125
- kv_cache: bfloat16 [2048, 2, 8, 128, 128], P('blk', None, 'kv')
- lengths: int32 [2], replicated, may hold values from 1 to 16384, as said below
- tables: int32 [16, 128], replicated, may hold values from 0 to 2047, as said below
- parents: int32 [4, 16], replicated, may hold values from 0 to 15, as said below
- routes: int32 [4, 16, 2], replicated, may hold values from 0 to 7, all different within a row; in each aligned block of 16 rows (0 to 15, 16 to 31, ..., all dimensions but the last counted through in order) at most 6 rows name the same one
Outputs:
- layer_out: bfloat16 [4, 16, 4096], P(None, None, 'blk')
Inputs may be any that keep to these rules, and one draw needn't show every extreme that they name: `lengths`: one group has exactly 16384 cached positions. `tables`: each pool block is named exactly once. `parents`: a beam's parent is a beam of its own group of 8 consecutive beams. `routes`: in each step no expert is named by more than 6 beams, a bound that some block reaches.
All inputs are finite; a program needn't handle non-finite values.
Results may differ from a plain program's by a relative error of at most 0.013.
Values may be sent and summed in bfloat16 or wider, within the bound.
No kernel may reach another device: no remote copies, remote signals or barrier semaphores. Data moves between devices by JAX's collectives and lax.ppermute only.
A program may use at most 64 MiB of HBM per device.

v0:
```python
import math

import jax
import jax.numpy as jnp
from jax import lax
from jax.sharding import PartitionSpec as P

MODEL_WIDTH = 4096
HEAD_WIDTH = 128
QUERIES_PER_KEY = 4
EXPERTS = 8
BEAM_W = 8
GROUPS = 2
DECODE_STEPS = 4
BLOCK_POSITIONS = 128
BEAM_BLOCKS = 128
BEAM_TOTAL = 16
CAP = 6


NORM_FLOOR = 1e-05
ROPE_BASE = 1000000.0
NEG_FILL = -1e30


def joined(value, axis, join):
    pieces = jax.tree.map(lambda part: lax.all_gather(part, axis), value)
    head = jax.tree.map(lambda part: part[0], pieces)
    tail = jax.tree.map(lambda part: part[1:], pieces)
    running, _ = lax.scan(lambda running, section: (join(running, section), None), head, tail)
    return running


def rotate_pairs(vectors, positions):
    half_width = vectors.shape[-1] // 2
    exponents = jnp.arange(half_width, dtype=jnp.float32) * (2.0 / vectors.shape[-1])
    frequency = ROPE_BASE ** (-exponents)
    angles = positions.astype(jnp.float32)[..., None] * frequency
    cosine = jnp.cos(angles)
    sine_part = jnp.sin(angles)
    lower_half = vectors[..., :half_width]
    upper_half = vectors[..., half_width:]
    return jnp.concatenate(
        [
            lower_half * cosine - upper_half * sine_part,
            upper_half * cosine + lower_half * sine_part,
        ],
        axis=-1,
    )


def lineage(parents):
    steps_count, beam_count = parents.shape
    beam_ids = jnp.arange(beam_count, dtype=jnp.int32)
    line_rows = []
    anchor_rows = []
    for step_index in range(steps_count):
        current = beam_ids
        levels = [jnp.full((beam_count,), -1, jnp.int32) for level_index in range(steps_count)]
        for level_index in range(step_index, -1, -1):
            levels[level_index] = current
            current = parents[level_index][current]
        line_rows.append(jnp.stack(levels))
        anchor_rows.append(current)
    return (jnp.stack(line_rows), jnp.stack(anchor_rows))


def expert_rank(routes):
    steps_count, beam_count, pick_count = routes.shape
    onehot = (routes[..., None] == jnp.arange(EXPERTS, dtype=jnp.int32)).astype(jnp.int32)
    flat_hits = onehot.reshape(steps_count, beam_count * pick_count, EXPERTS)
    before = jnp.cumsum(flat_hits, axis=1) - flat_hits
    return jnp.sum(before * flat_hits, axis=-1).reshape(steps_count, beam_count, pick_count)


def head_total(partial_value):
    return lax.psum(partial_value, "kv")


def combine_parts(part_one, part_two):
    max_one, sum_one, vector_one = part_one
    max_two, sum_two, vector_two = part_two
    larger = jnp.maximum(max_one, max_two)
    scale_one = jnp.exp(max_one - larger)
    scale_two = jnp.exp(max_two - larger)
    return (
        larger,
        sum_one * scale_one + sum_two * scale_two,
        vector_one * scale_one[..., None] + vector_two * scale_two[..., None],
    )


def groups_to_beams(grouped):
    shaped = grouped.reshape((GROUPS, DECODE_STEPS, BEAM_W, QUERIES_PER_KEY) + grouped.shape[2:])
    shaped = jnp.moveaxis(shaped, 1, 0)
    return shaped.reshape((DECODE_STEPS, BEAM_TOTAL, QUERIES_PER_KEY) + grouped.shape[2:])


def body(
    hidden_in,
    attn_gain,
    ffn_gain,
    query_key_value_weight,
    out_weight,
    router_weight,
    expert_in,
    expert_down,
    kv_cache,
    lengths,
    tables,
    parents,
    routes,
):
    count_tokens = DECODE_STEPS * BEAM_TOTAL
    width_local = hidden_in.shape[2]
    heads_local = query_key_value_weight.shape[1]
    logit_scale = 1.0 / math.sqrt(HEAD_WIDTH)
    line_beams, anchor = lineage(parents)
    flat_in = hidden_in.reshape(count_tokens, width_local).astype(jnp.float32)
    pre_attn = (flat_in * attn_gain.astype(jnp.float32)).astype(jnp.bfloat16)
    partial_proj = jnp.dot(
        pre_attn,
        query_key_value_weight.reshape(width_local, -1),
        preferred_element_type=jnp.float32,
    )
    partial_sq = jnp.sum(flat_in * flat_in, axis=1)
    projected_rows, square_sum = lax.psum((partial_proj, partial_sq), "blk")
    projected_rows = (
        projected_rows * lax.rsqrt(square_sum / MODEL_WIDTH + NORM_FLOOR)[:, None]
    ).reshape(DECODE_STEPS, BEAM_TOTAL, heads_local, QUERIES_PER_KEY + 2, HEAD_WIDTH)
    beam_groups = jnp.arange(BEAM_TOTAL, dtype=jnp.int32) // BEAM_W
    positions = lengths[beam_groups][None, :] + jnp.arange(DECODE_STEPS, dtype=jnp.int32)[:, None]
    queries = rotate_pairs(
        projected_rows[:, :, :, :QUERIES_PER_KEY], positions[:, :, None, None]
    ).astype(jnp.bfloat16)
    new_key = rotate_pairs(projected_rows[:, :, :, QUERIES_PER_KEY], positions[:, :, None]).astype(
        jnp.bfloat16
    )
    new_value = projected_rows[:, :, :, QUERIES_PER_KEY + 1].astype(jnp.bfloat16)
    slot_count = kv_cache.shape[0]
    slot_base = lax.axis_index("blk") * slot_count
    entry_ids = jnp.arange(BEAM_TOTAL * BEAM_BLOCKS, dtype=jnp.int32)
    owner_all = (
        jnp.zeros((BEAM_TOTAL * BEAM_BLOCKS,), jnp.int32)
        .at[tables.reshape(-1)]
        .set(entry_ids // BEAM_BLOCKS)
    )
    block_all = (
        jnp.zeros((BEAM_TOTAL * BEAM_BLOCKS,), jnp.int32)
        .at[tables.reshape(-1)]
        .set(entry_ids % BEAM_BLOCKS)
    )
    owner_here = lax.dynamic_slice_in_dim(owner_all, slot_base, slot_count)
    block_here = lax.dynamic_slice_in_dim(block_all, slot_base, slot_count)
    group_here = owner_here // BEAM_W
    live_keys = (
        block_here[:, None] * BLOCK_POSITIONS
        + jnp.arange(BLOCK_POSITIONS, dtype=jnp.int32)[None, :]
        < lengths[group_here][:, None]
    )
    anchor_groups = jnp.moveaxis(anchor.reshape(DECODE_STEPS, GROUPS, BEAM_W), 1, 0)
    anchor_query = jnp.broadcast_to(
        anchor_groups[..., None], (GROUPS, DECODE_STEPS, BEAM_W, QUERIES_PER_KEY)
    ).reshape(GROUPS, -1)
    query_match = anchor_query[group_here] == owner_here[:, None]
    group_hits = group_here[:, None] == jnp.arange(GROUPS, dtype=jnp.int32)[None, :]
    group_float = group_hits.astype(jnp.float32)
    recent_allowed = jnp.transpose(
        line_beams[:, :, :, None] == jnp.arange(BEAM_TOTAL, dtype=jnp.int32), (0, 2, 1, 3)
    ).reshape(DECODE_STEPS, BEAM_TOTAL, 1, count_tokens)
    is_first = lax.axis_index("blk") == 0
    query_head = queries[:, :, 0]
    query_groups = jnp.moveaxis(
        query_head.reshape(DECODE_STEPS, GROUPS, BEAM_W, QUERIES_PER_KEY, HEAD_WIDTH), 1, 0
    ).reshape(GROUPS, -1, HEAD_WIDTH)
    query_slots = query_groups[group_here]
    key_matrix = kv_cache[:, 0, 0]
    value_matrix = kv_cache[:, 1, 0]
    scores = (
        jnp.einsum("ptd,pqd->ptq", key_matrix, query_slots, preferred_element_type=jnp.float32)
        * logit_scale
    )
    allowed = live_keys[:, :, None] & query_match[:, None, :]
    masked = jnp.where(allowed, scores, NEG_FILL)
    slot_max = jnp.max(masked, axis=1)
    weights = jnp.where(allowed, jnp.exp(masked - slot_max[:, None, :]), 0.0)
    slot_sum = jnp.sum(weights, axis=1)
    slot_vector = jnp.einsum(
        "ptq,ptd->pqd",
        weights.astype(jnp.bfloat16),
        value_matrix,
        preferred_element_type=jnp.float32,
    )
    group_max = jnp.max(jnp.where(group_hits[:, :, None], slot_max[:, None, :], NEG_FILL), axis=0)
    rescale = jnp.exp(slot_max - group_max[group_here])
    group_sum = jnp.einsum(
        "pg,pq->gq", group_float, slot_sum * rescale, precision=lax.Precision.HIGHEST
    )
    group_vector = jnp.einsum(
        "pg,pqd->gqd",
        group_float,
        slot_vector * rescale[:, :, None],
        precision=lax.Precision.HIGHEST,
    )
    cache_max = groups_to_beams(group_max)
    cache_sum = groups_to_beams(group_sum)
    cache_vector = groups_to_beams(group_vector)
    newest_keys = new_key[:, :, 0].reshape(count_tokens, HEAD_WIDTH)
    newest_values = new_value[:, :, 0].reshape(count_tokens, HEAD_WIDTH)
    newest_logits = (
        jnp.einsum("sbqd,kd->sbqk", query_head, newest_keys, preferred_element_type=jnp.float32)
        * logit_scale
    )
    recent_masked = jnp.where(recent_allowed, newest_logits, NEG_FILL)
    recent_max = jnp.max(recent_masked, axis=-1)
    recent_weights = jnp.where(recent_allowed, jnp.exp(recent_masked - recent_max[..., None]), 0.0)
    recent_sum = jnp.sum(recent_weights, axis=-1)
    recent_vector = jnp.einsum(
        "sbqk,kd->sbqd",
        recent_weights.astype(jnp.bfloat16),
        newest_values,
        preferred_element_type=jnp.float32,
    )
    recent_max = jnp.where(is_first, recent_max, NEG_FILL)
    recent_sum = jnp.where(is_first, recent_sum, 0.0)
    recent_vector = jnp.where(is_first, recent_vector, 0.0)
    local_max, local_sum, local_vector = combine_parts(
        (cache_max, cache_sum, cache_vector), (recent_max, recent_sum, recent_vector)
    )
    max_heads = [local_max]
    sum_heads = [local_sum]
    vector_heads = [local_vector]
    part_max = jnp.stack(max_heads, axis=2)
    part_sum = jnp.stack(sum_heads, axis=2)
    part_vector = jnp.stack(vector_heads, axis=2)
    whole_max, whole_sum, whole_vector = joined(
        (part_max, part_sum, part_vector), "blk", combine_parts
    )
    attended_rows = (
        (whole_vector / whole_sum[..., None]).astype(jnp.bfloat16).reshape(count_tokens, -1)
    )
    attn_partial = jnp.dot(attended_rows, out_weight, preferred_element_type=jnp.float32)
    attn_out = head_total(attn_partial)
    residual = (flat_in + attn_out).astype(jnp.bfloat16)
    experts_local = expert_in.shape[0]
    ff_local = expert_in.shape[3]
    rows_per_expert = DECODE_STEPS * CAP
    rows_local = experts_local * rows_per_expert
    flat_routes = routes.reshape(count_tokens, 2)
    rank = expert_rank(routes).reshape(count_tokens, 2)
    step_of = jnp.arange(count_tokens, dtype=jnp.int32) // BEAM_TOTAL
    row_id = (flat_routes * rows_per_expert + step_of[:, None] * CAP + rank).reshape(-1)
    token_ids = jnp.broadcast_to(
        jnp.arange(count_tokens, dtype=jnp.int32)[:, None], (count_tokens, 2)
    ).reshape(-1)
    table_size = EXPERTS * rows_per_expert
    row_token_all = jnp.zeros((table_size,), jnp.int32).at[row_id].set(token_ids)
    row_live_all = jnp.zeros((table_size,), jnp.float32).at[row_id].set(1.0)
    row_other_all = (
        jnp.zeros((table_size,), jnp.int32).at[row_id].set(flat_routes[:, ::-1].reshape(-1))
    )
    row_start = lax.axis_index("kv") * rows_local
    row_token = lax.dynamic_slice_in_dim(row_token_all, row_start, rows_local)
    row_live = lax.dynamic_slice_in_dim(row_live_all, row_start, rows_local)
    row_other = lax.dynamic_slice_in_dim(row_other_all, row_start, rows_local)
    row_own = (row_start + jnp.arange(rows_local, dtype=jnp.int32)) // rows_per_expert
    in_flat = expert_in.reshape(experts_local, MODEL_WIDTH, 2 * ff_local)
    gain_wide = ffn_gain.astype(jnp.float32)
    full_rows = lax.all_gather(residual, "blk", axis=1, tiled=True)
    chosen = full_rows[row_token].astype(jnp.float32)
    pre_rows = (chosen * gain_wide).astype(jnp.bfloat16)
    sums_in = jnp.einsum(
        "erd,edf->erf",
        pre_rows.reshape(experts_local, rows_per_expert, MODEL_WIDTH),
        in_flat,
        preferred_element_type=jnp.float32,
    )
    sums_router = jnp.dot(pre_rows, router_weight, preferred_element_type=jnp.float32)
    sum_sq = jnp.sum(chosen * chosen, axis=1)
    inv_rows = lax.rsqrt(sum_sq / MODEL_WIDTH + NORM_FLOOR)
    expert_act = sums_in * inv_rows.reshape(experts_local, rows_per_expert)[:, :, None]
    expert_hidden = (jax.nn.silu(expert_act[..., :ff_local]) * expert_act[..., ff_local:]).astype(
        jnp.bfloat16
    )
    down_part = jnp.einsum(
        "erf,efd->erd", expert_hidden, expert_down, preferred_element_type=jnp.float32
    ).reshape(rows_local, MODEL_WIDTH)
    expert_result = lax.psum_scatter(down_part, "blk", scatter_dimension=1, tiled=True)
    logits = sums_router * inv_rows[:, None]
    expert_ids = jnp.arange(EXPERTS, dtype=jnp.int32)
    own_logit = jnp.sum(jnp.where(row_own[:, None] == expert_ids[None, :], logits, 0.0), axis=1)
    other_logit = jnp.sum(jnp.where(row_other[:, None] == expert_ids[None, :], logits, 0.0), axis=1)
    gate_share = row_live / (1.0 + jnp.exp(other_logit - own_logit))
    weighted_values = expert_result * gate_share[:, None]
    placement = (row_token[None, :] == jnp.arange(count_tokens, dtype=jnp.int32)[:, None]).astype(
        jnp.float32
    )
    mixture_part = jnp.dot(placement, weighted_values, precision=lax.Precision.HIGHEST)
    mixture = head_total(mixture_part)
    layer_out = (residual.astype(jnp.float32) + mixture).astype(jnp.bfloat16)
    return layer_out.reshape(DECODE_STEPS, BEAM_TOTAL, width_local)


def solution(mesh):
    placed = (
        P(None, None, "blk"),
        P("blk"),
        P(),
        P("blk", "kv", None),
        P("kv", "blk"),
        P(),
        P("kv", None, None, "blk"),
        P("kv", "blk", None),
        P("blk", None, "kv", None, None),
        P(),
        P(),
        P(),
        P(),
    )
    return jax.shard_map(
        body, mesh=mesh, in_specs=placed, out_specs=P(None, None, "blk"), check_vma=False
    )
```

profile of v0, /device:TPU:2, one launch (start us, length us, event | category | flops | bytes accessed | tf_op | source)
XLA Modules:
  0.0 434.0 jit_solution(2719535748926274330)
XLA Ops:
  8.2 1.8 fusion.31
  10.0 1.3 fusion.108
  12.1 8.0 %scatter_custom_fusion = s32[2048]{0:T(1024)S(1)} fusion(s32[2048]{0:T(1024)S(1)} %bitcast.249, s32[2048]{0:T(1024)S(1)} %add_select_fusion, s32[]{:T(128)} %constant.125.clone.1), kind=kCustom, calls=%fused_computation.168 | custom fusion | bytes 8196 | tf_op jit(solution)/shard_map/scatter | solution.py:146
  20.1 8.0 %scatter_custom_fusion.1 = s32[2048]{0:T(1024)S(1)} fusion(s32[2048]{0:T(1024)S(1)} %bitcast.250, s32[2048]{0:T(1024)S(1)} %fusion.64, s32[]{:T(128)} %constant.125.clone.1), kind=kCustom, calls=%fused_computation.166 | custom fusion | bytes 8196 | tf_op jit(solution)/shard_map/scatter | solution.py:151
  28.2 1.3 fusion.86
  29.5 1.4 compare_select_fusion.12
  39.1 62.3 %psum.29 = f32[64]{0:T(128)S(1)} all-reduce(f32[64]{0:T(128)S(1)} %reduce_sum.66), channel_id=1, replica_groups=mesh['kv'=8,'blk'=32] {'blk'}, use_global_device_ids=true, to_apply=%region_4.5 | all-reduce | flops 64 | bytes 512 | tf_op jit(solution)/shard_map/psum | solution.py:127
  103.0 21.4 %all-reduce.2.cloned.1.call-done = f32[64,768]{1,0:T(8,128)} async-done(((f32[64,768]{1,0:T(8,128)}), f32[64,768]{1,0:T(8,128)}) %all-reduce.2.cloned.1.call-update) | async-done | bytes 196624 | tf_op jit(solution)/shard_map/psum | solution.py:127
  124.4 1.0 broadcast_multiply_fusion
  125.9 2.2 gather_fusion.11
  128.0 4.6 %fusion.8 = (f32[64,128]{1,0:T(8,128)S(1)}, f32[64,128,128]{1,2,0:T(8,128)}) fusion(pred[64,128]{1,0:T(8,128)(4,1)S(1)} %broadcast_compare_fusion.1, pred[64,128]{1,0:T(8,128)(4,1)S(1)} %add_compare_fusion, bf16[64,128,128]{2,1,0:T(8,128)(2,1)} %gather_fusion.11, bf16[64,2,1,128,128]{4,3,2,1,0:T(8,128)(2,1)} %param.23), kind=kOutput, calls=%fused_computation.35 | convolution fusion | flops 272621568 | bytes 8437760 | tf_op jit(solution)/shard_map/ptd,pqd->ptq/dot_general | solution.py:180
  133.9 5.8 %convolution_multiply_fusion = f32[64,128,128]{2,1,0:T(8,128)S(1)} fusion(f32[64,128,128]{1,2,0:T(8,128)} %get-tuple-element.131, f32[64,128]{1,0:T(8,128)S(1)} %subtract_exponential_fusion.1, bf16[64,2,1,128,128]{4,3,2,1,0:T(8,128)(2,1)} %param.23, f32[64,128]{1,0:T(8,128)S(1)} %get-tuple-element.130, pred[64,128]{1,0:T(8,128)(4,1)S(1)} %broadcast_compare_fusion.1, ...), kind=kOutput, calls=%fused_computation.38 | convolution fusion | flops 275775488 | bytes 10567680 | tf_op jit(solution)/shard_map/ptq,ptd->pqd/dot_general | solution.py:188
  139.8 3.8 fusion.6
  146.4 4.9 %copy.153 = bf16[512,8,2,256]{3,1,2,0:T(8,128)(2,1)} copy(bf16[512,8,2,256]{3,2,1,0:T(2,128)(2,1)} %bitcast.232) | data formatting | bytes 8388608
  151.2 1.0 scatter_custom_fusion.2
  152.4 3.8 fusion.10
  157.0 22.3 %all_gather.13 = f32[32,4,16,1,4]{2,4,3,1,0:T(4,128)S(1)} all-gather(f32[1,4,16,1,4]{2,4,3,1,0:T(4,128)S(1)} %get-tuple-element.113), channel_id=1, replica_groups=mesh['kv'=8,'blk'=32] {'blk'}, dimensions={0}, use_global_device_ids=true | all-gather | bytes 33792 | tf_op jit(solution)/shard_map/all_gather | solution.py:27
  179.3 24.4 %all_gather.12 = f32[32,4,16,1,4]{2,4,3,1,0:T(4,128)S(1)} all-gather(f32[1,4,16,1,4]{2,4,3,1,0:T(4,128)S(1)} %get-tuple-element.114), channel_id=1, replica_groups=mesh['kv'=8,'blk'=32] {'blk'}, dimensions={0}, use_global_device_ids=true | all-gather | bytes 33792 | tf_op jit(solution)/shard_map/all_gather | solution.py:27
  203.8 0.9 slice_bitcast_fusion.2
  204.7 4.7 %slice.137 = f32[124,16,4,128]{3,1,2,0:T(8,128)} slice(f32[128,16,4,128]{3,1,2,0:T(8,128)} %all-gather.3.cloned.1.call-done), slice={[4:128], [0:16], [0:4], [0:128]} | slice | bytes 8126464 | tf_op jit(solution)/shard_map/slice | solution.py:29
  209.4 50.2 %while.14 = (s32[]{:T(128)}, f32[4,16,1,4]{1,3,2,0:T(4,128)S(1)}, f32[4,16,1,4]{1,3,2,0:T(4,128)S(1)}, f32[4,16,1,4,128]{4,3,2,1,0:T(4,128)S(1)}, f32[31,4,16,1,...) while((s32[]{:T(128)}, f32[4,16,1,4]{1,3,2,0:T(4,128)S(1)}, ...), condition=%wide.region_11.12_spmd, body=%wide.region_10.11_spmd.sunk | while | flops 100098 | bytes 674921 | solution.py:30
  209.7 0.9 constant_dynamic-slice_fusion.2
  211.3 0.9 constant_dynamic-slice_fusion.2
  212.9 0.9 constant_dynamic-slice_fusion.2
  214.5 0.9 constant_dynamic-slice_fusion.2
  216.1 0.9 constant_dynamic-slice_fusion.2
  217.8 0.9 constant_dynamic-slice_fusion.2
  221.0 0.9 constant_dynamic-slice_fusion.2
  222.6 0.9 constant_dynamic-slice_fusion.2
  224.2 0.9 constant_dynamic-slice_fusion.2
  225.9 0.9 constant_dynamic-slice_fusion.2
  227.5 0.9 constant_dynamic-slice_fusion.2
  229.1 0.9 constant_dynamic-slice_fusion.2
  230.7 0.9 constant_dynamic-slice_fusion.2
  232.3 0.9 constant_dynamic-slice_fusion.2
  233.9 0.9 constant_dynamic-slice_fusion.2
  235.6 0.9 constant_dynamic-slice_fusion.2
  238.8 0.9 constant_dynamic-slice_fusion.2
  240.4 0.9 constant_dynamic-slice_fusion.2
  242.0 0.9 constant_dynamic-slice_fusion.2
  260.0 30.2 %psum.30 = f32[64,128]{1,0:T(8,128)S(1)} all-reduce(f32[64,128]{1,0:T(8,128)S(1)} %fusion.38), channel_id=1, replica_groups=mesh['kv'=8,'blk'=32] {'kv'}, use_global_device_ids=true, to_apply=%region_12.13 | all-reduce | flops 8192 | bytes 65536 | tf_op jit(solution)/shard_map/psum | solution.py:77
  290.2 22.5 %all_gather.15 = bf16[64,4096]{1,0:T(8,128)(2,1)S(1)} all-gather(bf16[64,128]{1,0:T(8,128)(2,1)S(1)} %fusion.56), channel_id=1, replica_groups=mesh['kv'=8,'blk'=32] {'blk'}, dimensions={1}, use_global_device_ids=true | all-gather | bytes 540672 | tf_op jit(solution)/shard_map/all_gather | solution.py:269
  313.6 2.8 fusion.28
  316.5 1.1 fusion.15
  318.0 1.0 scatter_custom_fusion.4
  319.1 1.0 scatter_custom_fusion.3
  320.3 75.3 %reduce-scatter.2.cloned.1.call-done = f32[24,128]{1,0:T(8,128)} async-done(((f32[24,4096]{1,0:T(8,128)}), f32[24,128]{1,0:T(8,128)}) %reduce-scatter.2.cloned.1.call-update) | async-done | bytes 12304 | tf_op jit(solution)/shard_map/reduce_scatter | solution.py:288
  396.6 30.2 %psum.31 = f32[64,128]{1,0:T(8,128)S(1)} all-reduce(f32[64,128]{1,0:T(8,128)S(1)} %fusion.59), channel_id=1, replica_groups=mesh['kv'=8,'blk'=32] {'kv'}, use_global_device_ids=true, to_apply=%region_22.23 | all-reduce | flops 8192 | bytes 65536 | tf_op jit(solution)/shard_map/psum | solution.py:77
  (349 shorter events, 52.8 us)
Async XLA Ops:
  6.5 309.9 %copy-start = (bf16[1,256,4096]{2,1,0:T(8,128)(2,1)S(1)}, bf16[1,256,4096]{2,1,0:T(8,128)(2,1)}, u32[]{:S(2)}) copy-start(bf16[1,256,4096]{2,1,0:T(8,128)(2,1)} %param.22) | copy-start | bytes 6291460
  6.5 117.8 %all-reduce.2.cloned.1.call-start = ((), (), s32[]{:S(2)}) async-start(), calls=%async_computation.1 | async-start | bytes 393216 | tf_op jit(solution)/shard_map/psum | solution.py:127
  10.0 193.8 %all-gather.3.cloned.1.call-start = ((), (), s32[]{:S(2)}) async-start(), calls=%async_computation.3 | async-start | bytes 4325376 | tf_op jit(solution)/shard_map/all_gather | solution.py:27
  139.7 5.3 %copy-start.4 = (bf16[4096]{0:T(1024)(128)(2,1)S(1)}, bf16[4096]{0:T(1024)(128)(2,1)}, u32[]{:S(2)}) copy-start(bf16[4096]{0:T(1024)(128)(2,1)} %param.17) | copy-start | bytes 24580
  139.7 5.3 %copy-start.3 = (s32[4,16,2]{1,2,0:T(2,128)S(1)}, s32[4,16,2]{1,2,0:T(2,128)}, u32[]{:S(2)}) copy-start(s32[4,16,2]{1,2,0:T(2,128)} %param.27) | copy-start | bytes 1540
  144.8 250.9 %reduce-scatter.2.cloned.1.call-start = ((), (), s32[]{:S(2)}) async-start(), calls=%async_computation.2 | async-start | bytes 405504 | tf_op jit(solution)/shard_map/reduce_scatter | solution.py:288
  209.4 50.4 %copy-start.1 = (bf16[512,128]{1,0:T(8,128)(2,1)S(1)}, bf16[512,128]{1,0:T(8,128)(2,1)}, u32[]{:S(2)}) copy-start(bf16[512,128]{1,0:T(8,128)(2,1)} %param.19) | copy-start | bytes 393220
  209.4 80.8 %copy-start.2 = (bf16[4,16,128]{2,1,0:T(8,128)(2,1)S(1)}, bf16[4,16,128]{2,1,0:T(8,128)(2,1)}, u32[]{:S(2)}) copy-start(bf16[4,16,128]{2,1,0:T(8,128)(2,1)} %param.15) | copy-start | bytes 49156
  313.4 6.6 %copy-start.5 = (bf16[4096,8]{0,1:T(8,128)(2,1)S(1)}, bf16[4096,8]{0,1:T(8,128)(2,1)}, u32[]{:S(2)}) copy-start(bf16[4096,8]{0,1:T(8,128)(2,1)} %param.20) | copy-start | bytes 196612
Sparse Core Ops, SparseCore 0:
  10.6 113.7 all-reduce.1
  144.9 49.8 all-gather.2
  317.7 77.8 reduce-scatter.1
where the time goes:
time: 435 us; the launch traced here: 434 us
  blocking collectives  192 us (44%)
  waiting for transfers between devices  96.8 us (22%)
  local copies, waits for them, and re-layouts  80.5 us (19%)
  other arithmetic  27.1 us (6%)
  matrix products  22.6 us (5%)
  between operations  13.7 us (3%)
    reduce_scatter x1, waiting for transfers between devices, body(): lax.psum_scatter(down_part, 'blk', scatter_dimension=1, tiled=True)  75.3 us
    psum x1, blocking collectives, body(): projected_rows, square_sum = lax.psum((partial_proj, partial_sq), 'blk')  62.3 us
    psum x2, blocking collectives, head_total(): return lax.psum(partial_value, 'kv')  60.4 us
    all_gather x2, blocking collectives, joined(): pieces = jax.tree.map(lambda part: lax.all_gather(part, axis), value)  46.7 us
    dynamic_slice x31, local copies, waits for them, and re-layouts, joined(): lax.scan(lambda running, section: (join(running, section), None), head, t...  28.3 us
    all_gather x1, blocking collectives, body(): full_rows = lax.all_gather(residual, 'blk', axis=1, tiled=True)  22.5 us
    psum x1, waiting for transfers between devices, body(): projected_rows, square_sum = lax.psum((partial_proj, partial_sq), 'blk')  21.4 us
    add x31, other arithmetic, combine_parts(): vector_one * scale_one[..., None] + vector_two * scale_two[..., None]  13.1 us
  transfers between devices with their start and end apart: 3, of which 2 were waited for; matrix products, arithmetic and copies ran while one was open for 10% of the time, Pallas kernels for 0%

commit v1 on v0

--- a/solution.py
+++ b/solution.py
@@ -23,12 +23,49 @@
 NEG_FILL = -1e30
 
 
-def joined(value, axis, join):
-    pieces = jax.tree.map(lambda part: lax.all_gather(part, axis), value)
-    head = jax.tree.map(lambda part: part[0], pieces)
-    tail = jax.tree.map(lambda part: part[1:], pieces)
-    running, _ = lax.scan(lambda running, section: (join(running, section), None), head, tail)
-    return running
+def exchange(value, axis, size, distance):
+    pairs = [(index, index ^ distance) for index in range(size)]
+    return jax.tree.map(lambda part: lax.ppermute(part, axis, pairs), value)
+
+
+def butterfly(value, axis, size, join):
+    distance = 1
+    while distance < size:
+        value = join(value, exchange(value, axis, size, distance))
+        distance *= 2
+    return value
+
+
+def add_parts(first, second):
+    return jax.tree.map(lambda one, two: one + two, first, second)
+
+
+def gather_doubling(block, axis, size, dim):
+    index = lax.axis_index(axis)
+    distance = 1
+    while distance < size:
+        other = exchange(block, axis, size, distance)
+        upper = (index // distance) % 2 == 1
+        block = jnp.where(
+            upper,
+            jnp.concatenate([other, block], dim),
+            jnp.concatenate([block, other], dim),
+        )
+        distance *= 2
+    return block
+
+
+def scatter_halving(value, axis, size, dim):
+    index = lax.axis_index(axis)
+    distance = size // 2
+    while distance >= 1:
+        half = value.shape[dim] // 2
+        bit = (index // distance) % 2
+        keep = lax.dynamic_slice_in_dim(value, bit * half, half, dim)
+        send = lax.dynamic_slice_in_dim(value, (1 - bit) * half, half, dim)
+        value = keep + exchange(send, axis, size, distance)
+        distance //= 2
+    return value
 
 
 def rotate_pairs(vectors, positions):
@@ -73,8 +110,8 @@
     return jnp.sum(before * flat_hits, axis=-1).reshape(steps_count, beam_count, pick_count)
 
 
-def head_total(partial_value):
-    return lax.psum(partial_value, "kv")
+def head_total(partial_value, kv_size):
+    return butterfly(partial_value, "kv", kv_size, add_parts)
 
 
 def combine_parts(part_one, part_two):
@@ -110,6 +147,8 @@
     tables,
     parents,
     routes,
+    kv_size,
+    blk_size,
 ):
     count_tokens = DECODE_STEPS * BEAM_TOTAL
     width_local = hidden_in.shape[2]
@@ -124,7 +163,11 @@
         preferred_element_type=jnp.float32,
     )
     partial_sq = jnp.sum(flat_in * flat_in, axis=1)
-    projected_rows, square_sum = lax.psum((partial_proj, partial_sq), "blk")
+    packed_proj = butterfly(
+        jnp.concatenate([partial_proj, partial_sq[:, None]], axis=1), "blk", blk_size, add_parts
+    )
+    projected_rows = packed_proj[:, :-1]
+    square_sum = packed_proj[:, -1]
     projected_rows = (
         projected_rows * lax.rsqrt(square_sum / MODEL_WIDTH + NORM_FLOOR)[:, None]
     ).reshape(DECODE_STEPS, BEAM_TOTAL, heads_local, QUERIES_PER_KEY + 2, HEAD_WIDTH)
@@ -140,18 +183,11 @@
     slot_count = kv_cache.shape[0]
     slot_base = lax.axis_index("blk") * slot_count
     entry_ids = jnp.arange(BEAM_TOTAL * BEAM_BLOCKS, dtype=jnp.int32)
-    owner_all = (
-        jnp.zeros((BEAM_TOTAL * BEAM_BLOCKS,), jnp.int32)
-        .at[tables.reshape(-1)]
-        .set(entry_ids // BEAM_BLOCKS)
-    )
-    block_all = (
-        jnp.zeros((BEAM_TOTAL * BEAM_BLOCKS,), jnp.int32)
-        .at[tables.reshape(-1)]
-        .set(entry_ids % BEAM_BLOCKS)
-    )
-    owner_here = lax.dynamic_slice_in_dim(owner_all, slot_base, slot_count)
-    block_here = lax.dynamic_slice_in_dim(block_all, slot_base, slot_count)
+    slot_ids = slot_base + jnp.arange(slot_count, dtype=jnp.int32)
+    slot_hits = tables.reshape(-1)[None, :] == slot_ids[:, None]
+    entry_here = jnp.sum(jnp.where(slot_hits, entry_ids[None, :], 0), axis=1)
+    owner_here = entry_here // BEAM_BLOCKS
+    block_here = entry_here % BEAM_BLOCKS
     group_here = owner_here // BEAM_W
     live_keys = (
         block_here[:, None] * BLOCK_POSITIONS
@@ -233,14 +269,29 @@
     part_max = jnp.stack(max_heads, axis=2)
     part_sum = jnp.stack(sum_heads, axis=2)
     part_vector = jnp.stack(vector_heads, axis=2)
-    whole_max, whole_sum, whole_vector = joined(
-        (part_max, part_sum, part_vector), "blk", combine_parts
-    )
+    part_shape = part_max.shape
+    vector_rows = part_vector.reshape(-1, HEAD_WIDTH)
+    stat_rows = jnp.stack([part_max.reshape(-1), part_sum.reshape(-1)]).reshape(-1, HEAD_WIDTH)
+
+    def packed_combine(first, second):
+        def unpack(packed):
+            stats = packed[vector_rows.shape[0] :].reshape(2, -1)
+            return stats[0], stats[1], packed[: vector_rows.shape[0]]
+
+        larger, total, vector = combine_parts(unpack(first), unpack(second))
+        stats = jnp.stack([larger, total]).reshape(-1, HEAD_WIDTH)
+        return jnp.concatenate([vector, stats], axis=0)
+
+    whole_packed = butterfly(
+        jnp.concatenate([vector_rows, stat_rows], axis=0), "blk", blk_size, packed_combine
+    )
+    whole_vector = whole_packed[: vector_rows.shape[0]].reshape(part_vector.shape)
+    whole_sum = whole_packed[vector_rows.shape[0] :].reshape(2, -1)[1].reshape(part_shape)
     attended_rows = (
         (whole_vector / whole_sum[..., None]).astype(jnp.bfloat16).reshape(count_tokens, -1)
     )
     attn_partial = jnp.dot(attended_rows, out_weight, preferred_element_type=jnp.float32)
-    attn_out = head_total(attn_partial)
+    attn_out = head_total(attn_partial, kv_size)
     residual = (flat_in + attn_out).astype(jnp.bfloat16)
     experts_local = expert_in.shape[0]
     ff_local = expert_in.shape[3]
@@ -266,7 +317,7 @@
     row_own = (row_start + jnp.arange(rows_local, dtype=jnp.int32)) // rows_per_expert
     in_flat = expert_in.reshape(experts_local, MODEL_WIDTH, 2 * ff_local)
     gain_wide = ffn_gain.astype(jnp.float32)
-    full_rows = lax.all_gather(residual, "blk", axis=1, tiled=True)
+    full_rows = gather_doubling(residual, "blk", blk_size, 1)
     chosen = full_rows[row_token].astype(jnp.float32)
     pre_rows = (chosen * gain_wide).astype(jnp.bfloat16)
     sums_in = jnp.einsum(
@@ -285,7 +336,7 @@
     down_part = jnp.einsum(
         "erf,efd->erd", expert_hidden, expert_down, preferred_element_type=jnp.float32
     ).reshape(rows_local, MODEL_WIDTH)
-    expert_result = lax.psum_scatter(down_part, "blk", scatter_dimension=1, tiled=True)
+    expert_result = scatter_halving(down_part, "blk", blk_size, 1)
     logits = sums_router * inv_rows[:, None]
     expert_ids = jnp.arange(EXPERTS, dtype=jnp.int32)
     own_logit = jnp.sum(jnp.where(row_own[:, None] == expert_ids[None, :], logits, 0.0), axis=1)
@@ -296,7 +347,7 @@
         jnp.float32
     )
     mixture_part = jnp.dot(placement, weighted_values, precision=lax.Precision.HIGHEST)
-    mixture = head_total(mixture_part)
+    mixture = head_total(mixture_part, kv_size)
     layer_out = (residual.astype(jnp.float32) + mixture).astype(jnp.bfloat16)
     return layer_out.reshape(DECODE_STEPS, BEAM_TOTAL, width_local)
 
@@ -317,6 +368,12 @@
         P(),
         P(),
     )
+    kv_size = mesh.shape["kv"]
+    blk_size = mesh.shape["blk"]
+
+    def sized(*arrays):
+        return body(*arrays, kv_size, blk_size)
+
     return jax.shard_map(
-        body, mesh=mesh, in_specs=placed, out_specs=P(None, None, "blk"), check_vma=False
-    )
+        sized, mesh=mesh, in_specs=placed, out_specs=P(None, None, "blk"), check_vma=False
+    )

time: 435 us -> 194 us (0.45)
  blocking collectives: 192 us -> 0 us
  local copies, waits for them, and re-layouts: 80.5 us -> 27.3 us
  starting transfers between devices: 0.27 us -> 46.6 us
  other arithmetic: 27.1 us -> 13.5 us
  between operations: 13.7 us -> 1.09 us
  waiting for transfers between devices: 96.8 us -> 84.4 us
    psum x3 -> x0, blocking collectives: 123 us -> none  [the longest x1 62.3 us: body(): projected_rows, square_sum = lax.psum((partial_proj, partial_sq), 'blk')]
    ppermute x0 -> x26, waiting for transfers between devices: none -> 84.4 us  [exchange(): return jax.tree.map(lambda part: lax.ppermute(part, axis, pairs), value)]
    reduce_scatter x1 -> x0, waiting for transfers between devices: 75.3 us -> none  [body(): lax.psum_scatter(down_part, 'blk', scatter_dimension=1, tiled=True)]
    all_gather x3 -> x0, blocking collectives: 69.3 us -> none  [the longest x2 46.7 us: joined(): pieces = jax.tree.map(lambda part: lax.all_gather(part, axis), value)]
    ppermute x0 -> x26, starting transfers between devices: none -> 46.6 us  [exchange(): return jax.tree.map(lambda part: lax.ppermute(part, axis, pairs), value)]
    dynamic_slice x31 -> x5, local copies, waits for them, and re-layouts: 28.3 us -> 0.07 us  [scatter_halving(): send = lax.dynamic_slice_in_dim(value, (1 - bit) * half, half, dim)]
    psum x1 -> x0, waiting for transfers between devices: 21.4 us -> none  [body(): projected_rows, square_sum = lax.psum((partial_proj, partial_sq), 'blk')]
    scatter x2 -> x0, local copies, waits for them, and re-layouts: 16.1 us -> none  [the longest x1 8.05 us: body(): block_all = jnp.zeros((BEAM_TOTAL * BEAM_BLOCKS,), jnp.int32).at[tables.r...]
  transfers between devices with their start and end apart: 3 -> 26, of which waited for: 2 -> 24; matrix products, arithmetic and copies ran while one was open for 10% -> 14% of each run, Pallas kernels for 0% -> 0%
where the time goes in v1:
time: 194 us
  waiting for transfers between devices  84.4 us (44%)
  starting transfers between devices  46.6 us (24%)
  local copies, waits for them, and re-layouts  27.3 us (14%)
  matrix products  20.7 us (11%)
  other arithmetic  13.5 us (7%)
    ppermute x26, waiting for transfers between devices, exchange(): return jax.tree.map(lambda part: lax.ppermute(part, axis, pairs), value)  84.4 us
    ppermute x26, starting transfers between devices, exchange(): return jax.tree.map(lambda part: lax.ppermute(part, axis, pairs), value)  46.6 us
    dot_general x1, matrix products, body(): jnp.einsum('ptq,ptd->pqd', weights.astype(jnp.bfloat16), value_matrix, pr...  6.72 us
    gather x10, local copies, waits for them, and re-layouts, lineage(): current = parents[level_index][current]  6.62 us
    unnamed x18, local copies, waits for them, and re-layouts  5.03 us
    dot_general x1, matrix products, body(): jnp.einsum('ptd,pqd->ptq', key_matrix, query_slots, preferred_element_typ...  4.63 us
    reduce_sum x1, other arithmetic, body(): slot_sum = jnp.sum(weights, axis=1)  4 us
  transfers between devices with their start and end apart: 26, of which 24 were waited for; matrix products, arithmetic and copies ran while one was open for 14% of the time, Pallas kernels for 0%

profile of v1, /device:TPU:2, one launch (start us, length us, event | category | flops | bytes accessed | tf_op | source)
XLA Modules:
  0.0 193.5 jit_solution(16431873763193791194)
XLA Ops:
  3.1 1.3 fusion.124
  8.9 1.4 and_select_fusion.8
  10.3 1.3 fusion.93
  17.6 2.3 %collective-permute-start.1 = (f32[64,769]{1,0:T(8,128)S(1)}, f32[64,769]{1,0:T(8,128)S(1)}, u32[]{:S(2)}, u32[]{:S(2)}) collective-permute-start(f32[64,769]{1,0:T(8,128)S(1)} %fusion.116), channel_id=1, source_target_pairs={{0,2},{1,3},{2,0},{3,1},{4,6},{5,7},{6,4},{7,5},{8,10},{9,11},{10,... | collective-permute-start | bytes 590600 | tf_op jit(solution)/shard_map/ppermute | solution.py:28
  20.0 6.2 %collective-permute-done.1 = f32[64,769]{1,0:T(8,128)S(1)} collective-permute-done((f32[64,769]{1,0:T(8,128)S(1)}, f32[64,769]{1,0:T(8,128)S(1)}, u32[]{:S(2)}, u32[]{:S(2)}) %collective-permute-start.1) | collective-permute-done | bytes 196896 | tf_op jit(solution)/shard_map/ppermute | solution.py:28
  26.2 1.7 collective-permute-start.2
  27.9 7.3 %collective-permute-done.2 = f32[64,769]{1,0:T(8,128)S(1)} collective-permute-done((f32[64,769]{1,0:T(8,128)S(1)}, f32[64,769]{1,0:T(8,128)S(1)}, u32[]{:S(2)}, u32[]{:S(2)}) %collective-permute-start.2) | collective-permute-done | bytes 196896 | tf_op jit(solution)/shard_map/ppermute | solution.py:28
  36.2 5.7 %collective-permute-done.3 = f32[64,769]{1,0:T(8,128)S(1)} collective-permute-done((f32[64,769]{1,0:T(8,128)S(1)}, f32[64,769]{1,0:T(8,128)S(1)}, u32[]{:S(2)}, u32[]{:S(2)}) %collective-permute-start.3) | collective-permute-done | bytes 196896 | tf_op jit(solution)/shard_map/ppermute | solution.py:28
  41.9 2.4 %collective-permute-start.4 = (f32[64,769]{1,0:T(8,128)S(1)}, f32[64,769]{1,0:T(8,128)S(1)}, u32[]{:S(2)}, u32[]{:S(2)}) collective-permute-start(f32[64,769]{1,0:T(8,128)S(1)} %add.552), channel_id=1, source_target_pairs={{0,16},{1,17},{2,18},{3,19},{4,20},{5,21},{6,22},{7,23},{8,24},{9,... | collective-permute-start | bytes 590600 | tf_op jit(solution)/shard_map/ppermute | solution.py:28
  44.3 5.4 %collective-permute-done.4 = f32[64,769]{1,0:T(8,128)S(1)} collective-permute-done((f32[64,769]{1,0:T(8,128)S(1)}, f32[64,769]{1,0:T(8,128)S(1)}, u32[]{:S(2)}, u32[]{:S(2)}) %collective-permute-start.4) | collective-permute-done | bytes 196896 | tf_op jit(solution)/shard_map/ppermute | solution.py:28
  50.4 2.2 %gather_fusion.11 = bf16[64,128,128]{2,1,0:T(8,128)(2,1)} fusion(bf16[2,128,128]{2,1,0:T(8,128)(2,1)S(1)} %bitcast.232, s32[1024]{0:T(1024)S(1)} %pad_clamp_fusion.1), kind=kCustom, calls=%fused_computation.11 | custom fusion | bytes 4194560 | tf_op jit(solution)/shard_map/gather | solution.py:212
  52.6 4.6 %fusion.2 = (f32[64,128]{1,0:T(8,128)S(1)}, f32[64,128,128]{1,2,0:T(8,128)}) fusion(pred[64,128]{1,0:T(8,128)(4,1)S(1)} %broadcast_compare_fusion.1, pred[64,128]{1,0:T(8,128)(4,1)S(1)} %add_compare_fusion, bf16[64,128,128]{2,1,0:T(8,128)(2,1)} %gather_fusion.11, bf16[64,2,1,128,128]{4,3,2,1,0:T(8,128)(2,1)} %param.21), kind=kOutput, calls=%fused_computation.21 | convolution fusion | flops 272621568 | bytes 8437760 | tf_op jit(solution)/shard_map/ptd,pqd->ptq/dot_general | solution.py:216
  59.6 4.0 %fusion.3 = f32[64,128]{1,0:T(8,128)S(1)} fusion(f32[64,128,128]{1,2,0:T(8,128)} %get-tuple-element.71, f32[64,128]{1,0:T(8,128)S(1)} %get-tuple-element.70, pred[64,128]{1,0:T(8,128)(4,1)S(1)} %broadcast_compare_fusion.1, pred[64,128]{1,0:T(8,128)(4,1)S(1)} %add_compare_fusion), kind=kLoop, calls=%fused_computation.22 | loop fusion | flops 6283264 | bytes 4276224 | tf_op jit(solution)/shard_map/reduce_sum | solution.py:223
  63.6 6.7 %convolution_multiply_fusion = f32[64,128,128]{2,1,0:T(8,128)S(1)} fusion(f32[64,128,128]{1,2,0:T(8,128)S(1)} %copy-done.1, f32[64,128]{1,0:T(8,128)S(1)} %subtract_exponential_fusion, bf16[64,2,1,128,128]{4,3,2,1,0:T(8,128)(2,1)} %param.21, f32[64,128]{1,0:T(8,128)S(1)} %get-tuple-element.70, pred[64,128]{1,0:T(8,128)(4,1)S(1)} %broadcast_compare_fusion.1, ...), kind=kOutput, calls=%fused_computation.24 | convolution fusion | flops 275775488 | bytes 10567680 | tf_op jit(solution)/shard_map/ptq,ptd->pqd/dot_general | solution.py:224
  70.3 3.8 %fusion = f32[2,128,128]{2,0,1:T(2,128)S(1)} fusion(f32[64,128,128]{2,1,0:T(8,128)S(1)} %convolution_multiply_fusion, s32[64]{0:T(128)S(1)} %get-tuple-element.28), kind=kOutput, calls=%fused_computation.19 | convolution fusion | flops 25165952 | bytes 4325632 | tf_op jit(solution)/shard_map/pg,pqd->gqd/dot_general | solution.py:235
  75.2 1.1 collective-permute-done.5
  76.6 1.3 collective-permute-start.6
  77.9 4.5 %collective-permute-done.6 = f32[260,128]{1,0:T(8,128)S(1)} collective-permute-done((f32[260,128]{1,0:T(8,128)S(1)}, f32[260,128]{1,0:T(8,128)S(1)}, u32[]{:S(2)}, u32[]{:S(2)}) %collective-permute-start.6) | collective-permute-done | bytes 133152 | tf_op jit(solution)/shard_map/ppermute | solution.py:28
  82.6 1.1 collective-permute-start.7
  83.7 5.5 %collective-permute-done.7 = f32[260,128]{1,0:T(8,128)S(1)} collective-permute-done((f32[260,128]{1,0:T(8,128)S(1)}, f32[260,128]{1,0:T(8,128)S(1)}, u32[]{:S(2)}, u32[]{:S(2)}) %collective-permute-start.7) | collective-permute-done | bytes 133152 | tf_op jit(solution)/shard_map/ppermute | solution.py:28
  90.0 4.5 %collective-permute-done.8 = f32[260,128]{1,0:T(8,128)S(1)} collective-permute-done((f32[260,128]{1,0:T(8,128)S(1)}, f32[260,128]{1,0:T(8,128)S(1)}, u32[]{:S(2)}, u32[]{:S(2)}) %collective-permute-start.8) | collective-permute-done | bytes 133152 | tf_op jit(solution)/shard_map/ppermute | solution.py:28
  94.7 2.4 %collective-permute-start.9 = (f32[260,128]{1,0:T(8,128)S(1)}, f32[260,128]{1,0:T(8,128)S(1)}, u32[]{:S(2)}, u32[]{:S(2)}) collective-permute-start(f32[260,128]{1,0:T(8,128)S(1)} %pad_maximum_fusion.5), channel_id=1, source_target_pairs={{0,16},{1,17},{2,18},{3,19},{4,20},{5,21},{6,22},{7,23},{8,24},{9,... | collective-permute-start | bytes 399368 | tf_op jit(solution)/shard_map/ppermute | solution.py:28
  99.0 2.5 %collective-permute-done.9 = f32[260,128]{1,0:T(8,128)S(1)} collective-permute-done((f32[260,128]{1,0:T(8,128)S(1)}, f32[260,128]{1,0:T(8,128)S(1)}, u32[]{:S(2)}, u32[]{:S(2)}) %collective-permute-start.9) | collective-permute-done | bytes 133152 | tf_op jit(solution)/shard_map/ppermute | solution.py:28
  103.5 3.1 %collective-permute-done.10 = f32[64,128]{1,0:T(8,128)S(1)} collective-permute-done((f32[64,128]{1,0:T(8,128)S(1)}, f32[64,128]{1,0:T(8,128)S(1)}, u32[]{:S(2)}, u32[]{:S(2)}) %collective-permute-start.10) | collective-permute-done | bytes 32800 | tf_op jit(solution)/shard_map/ppermute | solution.py:28
  106.6 2.2 %collective-permute-start.11 = (f32[64,128]{1,0:T(8,128)S(1)}, f32[64,128]{1,0:T(8,128)S(1)}, u32[]{:S(2)}, u32[]{:S(2)}) collective-permute-start(f32[64,128]{1,0:T(8,128)S(1)} %add.579), channel_id=1, source_target_pairs={{0,64},{32,96},{64,0},{96,32},{128,192},{160,224},{192,128},{224,1... | collective-permute-start | bytes 98312 | tf_op jit(solution)/shard_map/ppermute | solution.py:28
  108.8 2.6 %collective-permute-done.11 = f32[64,128]{1,0:T(8,128)S(1)} collective-permute-done((f32[64,128]{1,0:T(8,128)S(1)}, f32[64,128]{1,0:T(8,128)S(1)}, u32[]{:S(2)}, u32[]{:S(2)}) %collective-permute-start.11) | collective-permute-done | bytes 32800 | tf_op jit(solution)/shard_map/ppermute | solution.py:28
  111.4 6.1 %collective-permute-start.12 = (f32[64,128]{1,0:T(8,128)S(1)}, f32[64,128]{1,0:T(8,128)S(1)}, u32[]{:S(2)}, u32[]{:S(2)}) collective-permute-start(f32[64,128]{1,0:T(8,128)S(1)} %add.580), channel_id=1, source_target_pairs={{0,128},{32,160},{64,192},{96,224},{128,0},{160,32},{192,64},{224,... | collective-permute-start | bytes 98312 | tf_op jit(solution)/shard_map/ppermute | solution.py:28
  117.6 1.9 collective-permute-done.12
  119.6 1.2 collective-permute-done.13
  120.7 1.4 collective-permute-start.14
  122.3 2.4 %collective-permute-done.14 = bf16[64,256]{1,0:T(8,128)(2,1)S(1)} collective-permute-done((bf16[64,256]{1,0:T(8,128)(2,1)S(1)}, bf16[64,256]{1,0:T(8,128)(2,1)S(1)}, u32[]{:S(2)}, u32[]{:S(2)}) %collective-permute-start.14) | collective-permute-done | bytes 32800 | tf_op jit(solution)/shard_map/ppermute | solution.py:28
  124.8 2.2 %collective-permute-start.15 = (bf16[64,512]{1,0:T(8,128)(2,1)S(1)}, bf16[64,512]{1,0:T(8,128)(2,1)S(1)}, u32[]{:S(2)}, u32[]{:S(2)}) collective-permute-start(bf16[64,512]{1,0:T(8,128)(2,1)S(1)} %maximum_select_fusion.3), channel_id=1, source_target_pairs={{0,4},{1,5},{2,6},{3,7},{4,0},{5,1},{6,2},{7,3},{8,12},{9,13},{10,... | collective-permute-start | bytes 196616 | tf_op jit(solution)/shard_map/ppermute | solution.py:28
  127.1 3.5 %collective-permute-done.15 = bf16[64,512]{1,0:T(8,128)(2,1)S(1)} collective-permute-done((bf16[64,512]{1,0:T(8,128)(2,1)S(1)}, bf16[64,512]{1,0:T(8,128)(2,1)S(1)}, u32[]{:S(2)}, u32[]{:S(2)}) %collective-permute-start.15) | collective-permute-done | bytes 65568 | tf_op jit(solution)/shard_map/ppermute | solution.py:28
  130.7 1.7 collective-permute-start.16
  133.2 2.5 %collective-permute-done.16 = bf16[64,1024]{1,0:T(8,128)(2,1)S(1)} collective-permute-done((bf16[64,1024]{1,0:T(8,128)(2,1)S(1)}, bf16[64,1024]{1,0:T(8,128)(2,1)S(1)}, u32[]{:S(2)}, u32[]{:S(2)}) %collective-permute-start.16) | collective-permute-done | bytes 131104 | tf_op jit(solution)/shard_map/ppermute | solution.py:28
  135.8 5.5 %collective-permute-start.17 = (bf16[64,2048]{1,0:T(8,128)(2,1)S(1)}, bf16[64,2048]{1,0:T(8,128)(2,1)S(1)}, u32[]{:S(2)}, u32[]{:S(2)}) collective-permute-start(bf16[64,2048]{1,0:T(8,128)(2,1)S(1)} %maximum_select_fusion.1), channel_id=1, source_target_pairs={{0,16},{1,17},{2,18},{3,19},{4,20},{5,21},{6,22},{7,23},{8,24},{9,... | collective-permute-start | bytes 786440 | tf_op jit(solution)/shard_map/ppermute | solution.py:28
  141.4 4.9 %copy.148 = bf16[512,8,2,256]{3,1,2,0:T(8,128)(2,1)} copy(bf16[512,8,2,256]{3,2,1,0:T(2,128)(2,1)} %bitcast.234) | data formatting | bytes 8388608
  148.4 2.8 %fusion.22 = f32[1,24,512]{2,1,0:T(8,128)S(1)} fusion(bf16[4096,512]{1,0:T(8,128)(2,1)} %bitcast.233, bf16[24,4096]{1,0:T(8,128)(2,1)S(1)} %gather_fusion.13, f32[4096]{0:T(1024)S(1)} %convert_element_type.111, f32[24]{0:T(128)S(1)} %add_rsqrt_fusion), kind=kOutput, calls=%fused_computation.44 | convolution fusion | flops 100970496 | bytes 4456544 | tf_op jit(solution)/shard_map/erd,edf->erf/dot_general | solution.py:323
  151.7 1.8 collective-permute-start.18
  153.5 6.5 %collective-permute-done.18 = f32[24,2048]{1,0:T(8,128)S(1)} collective-permute-done((f32[24,2048]{1,0:T(8,128)S(1)}, f32[24,2048]{1,0:T(8,128)S(1)}, u32[]{:S(2)}, u32[]{:S(2)}) %collective-permute-start.18) | collective-permute-done | bytes 196640 | tf_op jit(solution)/shard_map/ppermute | solution.py:28
  161.0 3.8 %collective-permute-done.19 = f32[24,1024]{1,0:T(8,128)S(1)} collective-permute-done((f32[24,1024]{1,0:T(8,128)S(1)}, f32[24,1024]{1,0:T(8,128)S(1)}, u32[]{:S(2)}, u32[]{:S(2)}) %collective-permute-start.19) | collective-permute-done | bytes 98336 | tf_op jit(solution)/shard_map/ppermute | solution.py:28
  164.8 2.2 %collective-permute-start.20 = (f32[24,512]{1,0:T(8,128)S(1)}, f32[24,512]{1,0:T(8,128)S(1)}, u32[]{:S(2)}, u32[]{:S(2)}) collective-permute-start(f32[24,512]{1,0:T(8,128)S(1)} %constant_dynamic-slice_fusion.2), channel_id=1, source_target_pairs={{0,4},{1,5},{2,6},{3,7},{4,0},{5,1},{6,2},{7,3},{8,12},{9,13},{10,... | collective-permute-start | bytes 147464 | tf_op jit(solution)/shard_map/ppermute | solution.py:28
  171.3 3.1 %collective-permute-done.21 = f32[24,256]{1,0:T(8,128)S(1)} collective-permute-done((f32[24,256]{1,0:T(8,128)S(1)}, f32[24,256]{1,0:T(8,128)S(1)}, u32[]{:S(2)}, u32[]{:S(2)}) %collective-permute-start.21) | collective-permute-done | bytes 24608 | tf_op jit(solution)/shard_map/ppermute | solution.py:28
  176.5 3.4 %collective-permute-done.23 = f32[64,128]{1,0:T(8,128)S(1)} collective-permute-done((f32[64,128]{1,0:T(8,128)S(1)}, f32[64,128]{1,0:T(8,128)S(1)}, u32[]{:S(2)}, u32[]{:S(2)}) %collective-permute-start.23) | collective-permute-done | bytes 32800 | tf_op jit(solution)/shard_map/ppermute | solution.py:28
  179.9 1.5 collective-permute-start.24
  181.4 3.6 %collective-permute-done.24 = f32[64,128]{1,0:T(8,128)S(1)} collective-permute-done((f32[64,128]{1,0:T(8,128)S(1)}, f32[64,128]{1,0:T(8,128)S(1)}, u32[]{:S(2)}, u32[]{:S(2)}) %collective-permute-start.24) | collective-permute-done | bytes 32800 | tf_op jit(solution)/shard_map/ppermute | solution.py:28
  185.1 5.8 %collective-permute-start.25 = (f32[64,128]{1,0:T(8,128)S(1)}, f32[64,128]{1,0:T(8,128)S(1)}, u32[]{:S(2)}, u32[]{:S(2)}) collective-permute-start(f32[64,128]{1,0:T(8,128)S(1)} %add.616), channel_id=1, source_target_pairs={{0,128},{32,160},{64,192},{96,224},{128,0},{160,32},{192,64},{224,... | collective-permute-start | bytes 98312 | tf_op jit(solution)/shard_map/ppermute | solution.py:28
  190.9 2.1 %collective-permute-done.25 = f32[64,128]{1,0:T(8,128)S(1)} collective-permute-done((f32[64,128]{1,0:T(8,128)S(1)}, f32[64,128]{1,0:T(8,128)S(1)}, u32[]{:S(2)}, u32[]{:S(2)}) %collective-permute-start.25) | collective-permute-done | bytes 32800 | tf_op jit(solution)/shard_map/ppermute | solution.py:28
  (252 shorter events, 35.4 us)
Async XLA Ops:
  0.0 151.2 %copy-start = (bf16[1,256,4096]{2,1,0:T(8,128)(2,1)S(1)}, bf16[1,256,4096]{2,1,0:T(8,128)(2,1)}, u32[]{:S(2)}) copy-start(bf16[1,256,4096]{2,1,0:T(8,128)(2,1)} %param.20) | copy-start | bytes 6291460
  2.8 14.7 %collective-permute-start = (f32[64,769]{1,0:T(8,128)S(1)}, f32[64,769]{1,0:T(8,128)S(1)}, u32[]{:S(2)}, u32[]{:S(2)}) collective-permute-start(f32[64,769]{1,0:T(8,128)S(1)} %pad_maximum_fusion), channel_id=1, source_target_pairs={{0,1},{1,0},{2,3},{3,2},{4,5},{5,4},{6,7},{7,6},{8,9},{9,8},{10,11... | collective-permute-start | bytes 590600 | tf_op jit(solution)/shard_map/ppermute | solution.py:28
  17.6 8.6 %collective-permute-start.1 = (f32[64,769]{1,0:T(8,128)S(1)}, f32[64,769]{1,0:T(8,128)S(1)}, u32[]{:S(2)}, u32[]{:S(2)}) collective-permute-start(f32[64,769]{1,0:T(8,128)S(1)} %fusion.116), channel_id=1, source_target_pairs={{0,2},{1,3},{2,0},{3,1},{4,6},{5,7},{6,4},{7,5},{8,10},{9,11},{10,... | collective-permute-start | bytes 590600 | tf_op jit(solution)/shard_map/ppermute | solution.py:28
  26.2 9.0 %collective-permute-start.2 = (f32[64,769]{1,0:T(8,128)S(1)}, f32[64,769]{1,0:T(8,128)S(1)}, u32[]{:S(2)}, u32[]{:S(2)}) collective-permute-start(f32[64,769]{1,0:T(8,128)S(1)} %add.550), channel_id=1, source_target_pairs={{0,4},{1,5},{2,6},{3,7},{4,0},{5,1},{6,2},{7,3},{8,12},{9,13},{10,... | collective-permute-start | bytes 590600 | tf_op jit(solution)/shard_map/ppermute | solution.py:28
  35.2 6.6 %collective-permute-start.3 = (f32[64,769]{1,0:T(8,128)S(1)}, f32[64,769]{1,0:T(8,128)S(1)}, u32[]{:S(2)}, u32[]{:S(2)}) collective-permute-start(f32[64,769]{1,0:T(8,128)S(1)} %add.551), channel_id=1, source_target_pairs={{0,8},{1,9},{2,10},{3,11},{4,12},{5,13},{6,14},{7,15},{8,0},{9,1},... | collective-permute-start | bytes 590600 | tf_op jit(solution)/shard_map/ppermute | solution.py:28
  41.9 7.8 %collective-permute-start.4 = (f32[64,769]{1,0:T(8,128)S(1)}, f32[64,769]{1,0:T(8,128)S(1)}, u32[]{:S(2)}, u32[]{:S(2)}) collective-permute-start(f32[64,769]{1,0:T(8,128)S(1)} %add.552), channel_id=1, source_target_pairs={{0,16},{1,17},{2,18},{3,19},{4,20},{5,21},{6,22},{7,23},{8,24},{9,... | collective-permute-start | bytes 590600 | tf_op jit(solution)/shard_map/ppermute | solution.py:28
  59.6 4.0 %copy-start.1 = (f32[64,128,128]{1,2,0:T(8,128)S(1)}, f32[64,128,128]{1,2,0:T(8,128)}, u32[]{:S(2)}) copy-start(f32[64,128,128]{1,2,0:T(8,128)} %get-tuple-element.71) | copy-start | bytes 12582916
  74.1 28.3 %copy-start.5 = (bf16[512,128]{1,0:T(8,128)(2,1)S(1)}, bf16[512,128]{1,0:T(8,128)(2,1)}, u32[]{:S(2)}) copy-start(bf16[512,128]{1,0:T(8,128)(2,1)} %param.17) | copy-start | bytes 393220
  74.1 45.3 %copy-start.2 = (bf16[4,16,128]{2,1,0:T(8,128)(2,1)S(1)}, bf16[4,16,128]{2,1,0:T(8,128)(2,1)}, u32[]{:S(2)}) copy-start(bf16[4,16,128]{2,1,0:T(8,128)(2,1)} %param.13) | copy-start | bytes 49156
  74.2 48.0 %copy-start.3 = (s32[4,16,2]{1,2,0:T(2,128)S(1)}, s32[4,16,2]{1,2,0:T(2,128)}, u32[]{:S(2)}) copy-start(s32[4,16,2]{1,2,0:T(2,128)} %param.25) | copy-start | bytes 1540
  74.3 67.0 %copy-start.4 = (bf16[4096]{0:T(1024)(128)(2,1)S(1)}, bf16[4096]{0:T(1024)(128)(2,1)}, u32[]{:S(2)}) copy-start(bf16[4096]{0:T(1024)(128)(2,1)} %param.15) | copy-start | bytes 24580
  74.9 1.4 collective-permute-start.5
  76.6 5.7 %collective-permute-start.6 = (f32[260,128]{1,0:T(8,128)S(1)}, f32[260,128]{1,0:T(8,128)S(1)}, u32[]{:S(2)}, u32[]{:S(2)}) collective-permute-start(f32[260,128]{1,0:T(8,128)S(1)} %pad_maximum_fusion.2), channel_id=1, source_target_pairs={{0,2},{1,3},{2,0},{3,1},{4,6},{5,7},{6,4},{7,5},{8,10},{9,11},{10,... | collective-permute-start | bytes 399368 | tf_op jit(solution)/shard_map/ppermute | solution.py:28
  82.6 6.6 %collective-permute-start.7 = (f32[260,128]{1,0:T(8,128)S(1)}, f32[260,128]{1,0:T(8,128)S(1)}, u32[]{:S(2)}, u32[]{:S(2)}) collective-permute-start(f32[260,128]{1,0:T(8,128)S(1)} %pad_maximum_fusion.3), channel_id=1, source_target_pairs={{0,4},{1,5},{2,6},{3,7},{4,0},{5,1},{6,2},{7,3},{8,12},{9,13},{10,... | collective-permute-start | bytes 399368 | tf_op jit(solution)/shard_map/ppermute | solution.py:28
  89.4 5.1 %collective-permute-start.8 = (f32[260,128]{1,0:T(8,128)S(1)}, f32[260,128]{1,0:T(8,128)S(1)}, u32[]{:S(2)}, u32[]{:S(2)}) collective-permute-start(f32[260,128]{1,0:T(8,128)S(1)} %pad_maximum_fusion.4), channel_id=1, source_target_pairs={{0,8},{1,9},{2,10},{3,11},{4,12},{5,13},{6,14},{7,15},{8,0},{9,1},... | collective-permute-start | bytes 399368 | tf_op jit(solution)/shard_map/ppermute | solution.py:28
  94.7 6.8 %collective-permute-start.9 = (f32[260,128]{1,0:T(8,128)S(1)}, f32[260,128]{1,0:T(8,128)S(1)}, u32[]{:S(2)}, u32[]{:S(2)}) collective-permute-start(f32[260,128]{1,0:T(8,128)S(1)} %pad_maximum_fusion.5), channel_id=1, source_target_pairs={{0,16},{1,17},{2,18},{3,19},{4,20},{5,21},{6,22},{7,23},{8,24},{9,... | collective-permute-start | bytes 399368 | tf_op jit(solution)/shard_map/ppermute | solution.py:28
  102.6 4.0 %collective-permute-start.10 = (f32[64,128]{1,0:T(8,128)S(1)}, f32[64,128]{1,0:T(8,128)S(1)}, u32[]{:S(2)}, u32[]{:S(2)}) collective-permute-start(f32[64,128]{1,0:T(8,128)S(1)} %fusion.44), channel_id=1, source_target_pairs={{0,32},{32,0},{64,96},{96,64},{128,160},{160,128},{192,224},{224,1... | collective-permute-start | bytes 98312 | tf_op jit(solution)/shard_map/ppermute | solution.py:28
  106.6 4.8 %collective-permute-start.11 = (f32[64,128]{1,0:T(8,128)S(1)}, f32[64,128]{1,0:T(8,128)S(1)}, u32[]{:S(2)}, u32[]{:S(2)}) collective-permute-start(f32[64,128]{1,0:T(8,128)S(1)} %add.579), channel_id=1, source_target_pairs={{0,64},{32,96},{64,0},{96,32},{128,192},{160,224},{192,128},{224,1... | collective-permute-start | bytes 98312 | tf_op jit(solution)/shard_map/ppermute | solution.py:28
  111.4 8.0 %collective-permute-start.12 = (f32[64,128]{1,0:T(8,128)S(1)}, f32[64,128]{1,0:T(8,128)S(1)}, u32[]{:S(2)}, u32[]{:S(2)}) collective-permute-start(f32[64,128]{1,0:T(8,128)S(1)} %add.580), channel_id=1, source_target_pairs={{0,128},{32,160},{64,192},{96,224},{128,0},{160,32},{192,64},{224,... | collective-permute-start | bytes 98312 | tf_op jit(solution)/shard_map/ppermute | solution.py:28
  119.5 1.3 collective-permute-start.13
  120.7 4.0 %collective-permute-start.14 = (bf16[64,256]{1,0:T(8,128)(2,1)S(1)}, bf16[64,256]{1,0:T(8,128)(2,1)S(1)}, u32[]{:S(2)}, u32[]{:S(2)}) collective-permute-start(bf16[64,256]{1,0:T(8,128)(2,1)S(1)} %maximum_select_fusion.4), channel_id=1, source_target_pairs={{0,2},{1,3},{2,0},{3,1},{4,6},{5,7},{6,4},{7,5},{8,10},{9,11},{10,... | collective-permute-start | bytes 98312 | tf_op jit(solution)/shard_map/ppermute | solution.py:28
  124.8 5.9 %collective-permute-start.15 = (bf16[64,512]{1,0:T(8,128)(2,1)S(1)}, bf16[64,512]{1,0:T(8,128)(2,1)S(1)}, u32[]{:S(2)}, u32[]{:S(2)}) collective-permute-start(bf16[64,512]{1,0:T(8,128)(2,1)S(1)} %maximum_select_fusion.3), channel_id=1, source_target_pairs={{0,4},{1,5},{2,6},{3,7},{4,0},{5,1},{6,2},{7,3},{8,12},{9,13},{10,... | collective-permute-start | bytes 196616 | tf_op jit(solution)/shard_map/ppermute | solution.py:28
  130.7 5.1 %collective-permute-start.16 = (bf16[64,1024]{1,0:T(8,128)(2,1)S(1)}, bf16[64,1024]{1,0:T(8,128)(2,1)S(1)}, u32[]{:S(2)}, u32[]{:S(2)}) collective-permute-start(bf16[64,1024]{1,0:T(8,128)(2,1)S(1)} %maximum_select_fusion.2), channel_id=1, source_target_pairs={{0,8},{1,9},{2,10},{3,11},{4,12},{5,13},{6,14},{7,15},{8,0},{9,1},... | collective-permute-start | bytes 393224 | tf_op jit(solution)/shard_map/ppermute | solution.py:28
  135.8 11.6 %collective-permute-start.17 = (bf16[64,2048]{1,0:T(8,128)(2,1)S(1)}, bf16[64,2048]{1,0:T(8,128)(2,1)S(1)}, u32[]{:S(2)}, u32[]{:S(2)}) collective-permute-start(bf16[64,2048]{1,0:T(8,128)(2,1)S(1)} %maximum_select_fusion.1), channel_id=1, source_target_pairs={{0,16},{1,17},{2,18},{3,19},{4,20},{5,21},{6,22},{7,23},{8,24},{9,... | collective-permute-start | bytes 786440 | tf_op jit(solution)/shard_map/ppermute | solution.py:28
  148.4 22.7 %copy-start.6 = (bf16[4096,8]{0,1:T(8,128)(2,1)S(1)}, bf16[4096,8]{0,1:T(8,128)(2,1)}, u32[]{:S(2)}) copy-start(bf16[4096,8]{0,1:T(8,128)(2,1)} %param.18) | copy-start | bytes 196612
  151.7 8.3 %collective-permute-start.18 = (f32[24,2048]{1,0:T(8,128)S(1)}, f32[24,2048]{1,0:T(8,128)S(1)}, u32[]{:S(2)}, u32[]{:S(2)}) collective-permute-start(f32[24,2048]{1,0:T(8,128)S(1)} %constant_dynamic-slice_fusion.4), channel_id=1, source_target_pairs={{0,16},{1,17},{2,18},{3,19},{4,20},{5,21},{6,22},{7,23},{8,24},{9,... | collective-permute-start | bytes 589832 | tf_op jit(solution)/shard_map/ppermute | solution.py:28
  160.1 4.7 %collective-permute-start.19 = (f32[24,1024]{1,0:T(8,128)S(1)}, f32[24,1024]{1,0:T(8,128)S(1)}, u32[]{:S(2)}, u32[]{:S(2)}) collective-permute-start(f32[24,1024]{1,0:T(8,128)S(1)} %constant_dynamic-slice_fusion.3), channel_id=1, source_target_pairs={{0,8},{1,9},{2,10},{3,11},{4,12},{5,13},{6,14},{7,15},{8,0},{9,1},... | collective-permute-start | bytes 294920 | tf_op jit(solution)/shard_map/ppermute | solution.py:28
  164.8 5.7 %collective-permute-start.20 = (f32[24,512]{1,0:T(8,128)S(1)}, f32[24,512]{1,0:T(8,128)S(1)}, u32[]{:S(2)}, u32[]{:S(2)}) collective-permute-start(f32[24,512]{1,0:T(8,128)S(1)} %constant_dynamic-slice_fusion.2), channel_id=1, source_target_pairs={{0,4},{1,5},{2,6},{3,7},{4,0},{5,1},{6,2},{7,3},{8,12},{9,13},{10,... | collective-permute-start | bytes 147464 | tf_op jit(solution)/shard_map/ppermute | solution.py:28
  170.5 3.9 %collective-permute-start.21 = (f32[24,256]{1,0:T(8,128)S(1)}, f32[24,256]{1,0:T(8,128)S(1)}, u32[]{:S(2)}, u32[]{:S(2)}) collective-permute-start(f32[24,256]{1,0:T(8,128)S(1)} %constant_dynamic-slice_fusion.1), channel_id=1, source_target_pairs={{0,2},{1,3},{2,0},{3,1},{4,6},{5,7},{6,4},{7,5},{8,10},{9,11},{10,... | collective-permute-start | bytes 73736 | tf_op jit(solution)/shard_map/ppermute | solution.py:28
  174.4 1.3 collective-permute-start.22
  175.9 4.0 %collective-permute-start.23 = (f32[64,128]{1,0:T(8,128)S(1)}, f32[64,128]{1,0:T(8,128)S(1)}, u32[]{:S(2)}, u32[]{:S(2)}) collective-permute-start(f32[64,128]{1,0:T(8,128)S(1)} %fusion.61), channel_id=1, source_target_pairs={{0,32},{32,0},{64,96},{96,64},{128,160},{160,128},{192,224},{224,1... | collective-permute-start | bytes 98312 | tf_op jit(solution)/shard_map/ppermute | solution.py:28
  179.9 5.2 %collective-permute-start.24 = (f32[64,128]{1,0:T(8,128)S(1)}, f32[64,128]{1,0:T(8,128)S(1)}, u32[]{:S(2)}, u32[]{:S(2)}) collective-permute-start(f32[64,128]{1,0:T(8,128)S(1)} %add.615), channel_id=1, source_target_pairs={{0,64},{32,96},{64,0},{96,32},{128,192},{160,224},{192,128},{224,1... | collective-permute-start | bytes 98312 | tf_op jit(solution)/shard_map/ppermute | solution.py:28
  185.1 7.8 %collective-permute-start.25 = (f32[64,128]{1,0:T(8,128)S(1)}, f32[64,128]{1,0:T(8,128)S(1)}, u32[]{:S(2)}, u32[]{:S(2)}) collective-permute-start(f32[64,128]{1,0:T(8,128)S(1)} %add.616), channel_id=1, source_target_pairs={{0,128},{32,160},{64,192},{96,224},{128,0},{160,32},{192,64},{224,... | collective-permute-start | bytes 98312 | tf_op jit(solution)/shard_map/ppermute | solution.py:28
